TPU v7x, 32 devices: a whole 2x2x4 slice. The times are simulated.
32 devices in a mesh: dp: 4 (over z), ctx: 8 (over y, x, core).
Axes of the slice: x: 2, y: 2, z: 4, core: 2. Of those that a mesh axis runs over, the one named last changes fastest.
Arguments:
- tokens: bfloat16 [4, 1024, 6144], P('dp', 'ctx'), may hold values from -0.1875 to 0.1875
- cotangent: bfloat16 [4, 1024, 6144], P('dp', 'ctx'), may hold values from -6 to 6
- w_router: float32 [6144], replicated, may hold values from -2 to 2
- w_query: bfloat16 [6144, 4096], P(None, 'ctx'), may hold values from -0.078125 to 0.078125
- w_key: bfloat16 [6144, 4096], P(None, 'ctx'), may hold values from -0.078125 to 0.078125
- w_value: bfloat16 [6144, 4096], P(None, 'ctx'), may hold values from -0.078125 to 0.078125
- w_out: bfloat16 [4096, 6144], P('ctx'), may hold values from -0.09375 to 0.09375
- chosen: int32 [4, 160], P('dp', 'ctx'), may hold values from -1 to 1023, as said below
- counts: int32 [4, 8], P('dp', 'ctx'), may hold values from 12 to 20, as said below
Outputs:
- layer_out: bfloat16 [4, 1024, 6144], P('dp', 'ctx')
- grad_query: bfloat16 [6144, 4096], P('dp', 'ctx')
- grad_key: bfloat16 [6144, 4096], P('dp', 'ctx')
- grad_value: bfloat16 [6144, 4096], P('dp', 'ctx')
- grad_out: bfloat16 [4096, 6144], P('ctx', 'dp')
- grad_router: float32 [6144], replicated
Inputs may be any that keep to these rules, and one draw needn't show every extreme that they name: `chosen`: for every sequence b and device block c, the first counts[b, c] of the block's slots c * 20 to (c + 1) * 20 - 1 hold increasing positions of that device's tokens, c * 128 to (c + 1) * 128 - 1; the other slots hold -1. In every sequence the counts add up to 128, and some device's block has exactly 20 used slots.
All inputs are finite; a program needn't handle non-finite values.
Results may differ from a plain program's by a relative error of at most 0.018.
Values may be sent and summed in bfloat16 or wider, within the bound.
No kernel may reach another device: no remote copies, remote signals or barrier semaphores. Data moves between devices by JAX's collectives and lax.ppermute only.
A program may use at most 128 MiB of HBM per device.

v0:
```python
import math
import jax
import jax.numpy as jnp
from jax import lax
from jax.sharding import PartitionSpec as P

HDIM = 128
HIGHEST_PRECISION = lax.Precision.HIGHEST


def head_norm(values, width):
    shaped = values.reshape(values.shape[0], -1, width)
    inverse = lax.rsqrt(jnp.mean(shaped * shaped, axis=-1, keepdims=True) + 1e-06)
    return (shaped * inverse, inverse)


def norm_back(grad_hat, normal, inverse):
    return inverse * (grad_hat - normal * jnp.mean(grad_hat * normal, axis=-1, keepdims=True))


def rounded_term(part):
    return lax.optimization_barrier(part.astype(jnp.bfloat16)).astype(jnp.float32)


def body(n_dp, n_ctx, tokens, cotangent, w_router, w_query, w_key, w_value, w_out, chosen, counts):
    length = tokens.shape[1]
    width = tokens.shape[2]
    capacity = chosen.shape[1]
    inner = w_query.shape[1]
    heads_here = inner // HDIM
    scale = 1.0 / math.sqrt(HDIM)
    offset = lax.axis_index("ctx") * length
    slot_ids = lax.broadcasted_iota(jnp.int32, (capacity,), 0)
    local = chosen[0] - offset
    present = (slot_ids < counts[0, 0]) & (local >= 0) & (local < length)
    columns = lax.broadcasted_iota(jnp.int32, (capacity, length), 1)
    onehot = ((local[:, None] == columns) & present[:, None]).astype(jnp.bfloat16)
    rows = jnp.dot(onehot, tokens[0], preferred_element_type=jnp.float32)
    rows_back = jnp.dot(onehot, cotangent[0], preferred_element_type=jnp.float32)
    logits = jnp.dot(rows, w_router, precision=HIGHEST_PRECISION)
    weights = jax.nn.sigmoid(logits)
    normed = (rows * lax.rsqrt(jnp.mean(rows * rows, axis=-1, keepdims=True) + 1e-05)).astype(
        jnp.bfloat16
    )
    delta = (weights[:, None] * rows_back).astype(jnp.bfloat16)
    flag_cols = jnp.zeros((capacity, HDIM), jnp.bfloat16).at[:, 0].set(present.astype(jnp.bfloat16))
    packed = lax.all_gather(
        jnp.concatenate([normed, delta, flag_cols], axis=1), "ctx", axis=0, tiled=False
    )
    chunk_normed = packed[:, :, :width]
    chunk_delta = packed[:, :, width : 2 * width]
    all_present = packed[:, :, 2 * width].reshape(n_ctx * capacity)
    slots = n_ctx * capacity
    block = width // n_dp
    own_blocks = lax.all_to_all(jnp.concatenate([normed, delta], axis=0), "dp", 1, 0, tiled=True)
    pieces = lax.all_gather(own_blocks, "ctx", axis=0, tiled=False).reshape(
        n_ctx, n_dp, 2, capacity, block
    )
    normed_blocks = pieces[:, :, 0].transpose(1, 0, 2, 3).reshape(n_dp * slots, block)
    delta_blocks = pieces[:, :, 1].transpose(1, 0, 2, 3).reshape(n_dp * slots, block)

    def project(weight):
        raw = lax.dot_general(
            chunk_normed, weight, (((2,), (0,)), ((), ())), preferred_element_type=jnp.float32
        )
        return raw.reshape(slots, inner)

    query_raw = project(w_query)
    key_raw = project(w_key)
    value_raw = project(w_value)
    query_hat, query_scale = head_norm(query_raw, HDIM)
    key_hat, key_scale = head_norm(key_raw, HDIM)
    query_b = query_hat.astype(jnp.bfloat16)
    key_b = key_hat.astype(jnp.bfloat16)
    value_b = value_raw.reshape(slots, heads_here, HDIM).astype(jnp.bfloat16)
    current = lax.broadcasted_iota(jnp.int32, (slots, slots), 0)
    earlier = lax.broadcasted_iota(jnp.int32, (slots, slots), 1)
    allowed = (earlier <= current) & ((all_present[None, :] > 0.5) | (earlier == current))
    scores = jnp.einsum("ihd,jhd->hij", query_b, key_b, preferred_element_type=jnp.float32) * scale
    exponent = jnp.where(allowed[None], jnp.exp(scores), 0.0)
    attend = exponent / jnp.sum(exponent, axis=-1, keepdims=True)
    attend_b = attend.astype(jnp.bfloat16)
    mixed = jnp.einsum("hij,jhd->ihd", attend_b, value_b, preferred_element_type=jnp.float32)
    mixed = mixed.astype(jnp.bfloat16).reshape(slots, inner)
    mixed_back = lax.dot_general(
        chunk_delta, w_out, (((2,), (1,)), ((), ())), preferred_element_type=jnp.float32
    )
    mixed_back = mixed_back.astype(jnp.bfloat16).reshape(slots, heads_here, HDIM)
    attend_back = jnp.einsum(
        "ihd,jhd->hij", mixed_back, value_b, preferred_element_type=jnp.float32
    )
    inner_sum = jnp.sum(attend * attend_back, axis=-1, keepdims=True)
    scores_back = (attend * (attend_back - inner_sum) * scale).astype(jnp.bfloat16)
    value_back = jnp.einsum(
        "hij,ihd->jhd", attend_b, mixed_back, preferred_element_type=jnp.float32
    )
    value_back = value_back.astype(jnp.bfloat16).reshape(slots, inner)
    qhat_back = jnp.einsum("hij,jhd->ihd", scores_back, key_b, preferred_element_type=jnp.float32)
    khat_back = jnp.einsum("hij,ihd->jhd", scores_back, query_b, preferred_element_type=jnp.float32)
    query_back = (
        norm_back(qhat_back, query_hat, query_scale).astype(jnp.bfloat16).reshape(slots, inner)
    )
    key_back = norm_back(khat_back, key_hat, key_scale).astype(jnp.bfloat16).reshape(slots, inner)
    mixed_late, query_back, key_back, value_back = lax.optimization_barrier(
        (mixed, query_back, key_back, value_back)
    )
    contributions = lax.dot_general(
        mixed_late.reshape(n_ctx, capacity, inner),
        w_out,
        (((2,), (0,)), ((), ())),
        preferred_element_type=jnp.float32,
    ).astype(jnp.bfloat16)
    received = lax.all_to_all(contributions, "ctx", 0, 0, tiled=True)
    update = jnp.sum(received.astype(jnp.float32), axis=0)
    scaled = weights[:, None] * update
    spread = jnp.dot(onehot.astype(jnp.float32).T, scaled, precision=HIGHEST_PRECISION)
    layer_out = (tokens[0].astype(jnp.float32) + spread).astype(jnp.bfloat16)[None]
    gate_back = jnp.sum(rows_back * update, axis=-1) * weights * (1.0 - weights)
    router_part = jnp.dot(gate_back, rows, precision=HIGHEST_PRECISION)
    router_group = jnp.sum(lax.all_gather(router_part, "ctx", axis=0, tiled=False), axis=0)
    factors = lax.all_gather(
        jnp.concatenate([query_back, key_back, value_back], axis=1), "dp", axis=0, tiled=False
    ).reshape(n_dp * slots, 3 * inner)

    def contract(left, right):
        return lax.dot_general(
            left, right, (((0,), (0,)), ((), ())), preferred_element_type=jnp.float32
        ).astype(jnp.bfloat16)

    grads = contract(normed_blocks, factors)
    grad_query = grads[:, :inner]
    grad_key = grads[:, inner : 2 * inner]
    grad_value = grads[:, 2 * inner :]
    dp_index = lax.axis_index("dp")
    delta_by_seq = delta_blocks.reshape(n_dp, slots, block)
    out_total = lax.dot_general(
        mixed,
        lax.dynamic_index_in_dim(delta_by_seq, dp_index, 0, keepdims=False),
        (((0,), (0,)), ((), ())),
        preferred_element_type=jnp.float32,
    )
    for shift in range(1, n_dp):
        arrived = lax.ppermute(mixed, "dp", [(i, (i + shift) % n_dp) for i in range(n_dp)])
        source = (dp_index + n_dp - shift) % n_dp
        out_total = out_total + lax.dot_general(
            arrived,
            lax.dynamic_index_in_dim(delta_by_seq, source, 0, keepdims=False),
            (((0,), (0,)), ((), ())),
            preferred_element_type=jnp.float32,
        )
    grad_out = out_total.astype(jnp.bfloat16)
    router_pieces = lax.dynamic_update_index_in_dim(
        jnp.zeros((n_dp,) + router_group.shape, jnp.float32), router_group, dp_index, 0
    )
    for shift in range(1, n_dp):
        arrived = lax.ppermute(router_group, "dp", [(i, (i + shift) % n_dp) for i in range(n_dp)])
        router_pieces = lax.dynamic_update_index_in_dim(
            router_pieces, arrived, (dp_index + n_dp - shift) % n_dp, 0
        )
    grad_router = jnp.sum(router_pieces, axis=0)
    return (layer_out, grad_query, grad_key, grad_value, grad_out, grad_router)


def solution(mesh):
    n_dp = mesh.shape["dp"]
    n_ctx = mesh.shape["ctx"]
    in_specs = (
        P("dp", "ctx", None),
        P("dp", "ctx", None),
        P(),
        P(None, "ctx"),
        P(None, "ctx"),
        P(None, "ctx"),
        P("ctx", None),
        P("dp", "ctx"),
        P("dp", "ctx"),
    )
    out_specs = (
        P("dp", "ctx", None),
        P("dp", "ctx"),
        P("dp", "ctx"),
        P("dp", "ctx"),
        P("ctx", "dp"),
        P(),
    )

    def run(*args):
        return body(n_dp, n_ctx, *args)

    return jax.shard_map(run, mesh=mesh, in_specs=in_specs, out_specs=out_specs, check_vma=False)
```

profile of v0, /device:TPU:0, one launch (start us, length us, event | category | flops | bytes accessed | tf_op | source)
XLA Modules:
  0.0 164.5 jit_solution(2579473443318761461)
XLA Ops:
  7.2 0.6 compare_reduce_fusion.1
  8.5 0.7 compare_and_fusion
  9.2 1.9 %multiply_reduce_fusion.2 = (f32[20]{0:T(128)S(1)}, f32[20,6144]{1,0:T(8,128)S(1)}) fusion(bf16[1,128,6144]{2,1,0:T(8,128)(2,1)} %param.11, s32[20]{0:T(128)S(1)} %bitcast.142, pred[20]{0:T(512)(128)(4,1)S(1)} %get-tuple-element.26), kind=kOutput, calls=%fused_computation.61 | convolution fusion | flops 31708140 | bytes 2064564 | tf_op jit(solution)/shard_map/dot_general | solution.py:38
  11.1 1.4 fusion.44
  12.6 0.1 multiply_convert_fusion.1
  12.7 0.1 copy.127
  12.8 0.1 copy.128
  12.9 1.2 multiply_convert_fusion
  14.1 0.7 fusion.91
  14.8 0.9 fusion.50
  15.7 0.1 pad_maximum_fusion
  15.8 20.0 %all_to_all.21 = bf16[40,4,1536]{2,0,1:T(8,128)(2,1)} all-to-all(bf16[40,4,1536]{2,0,1:T(8,128)(2,1)S(1)} %bitcast.130), channel_id=1, replica_groups=mesh['dp'=4,'ctx'=8] {'dp'}, dimensions={1} | all-to-all | bytes 983040 | tf_op jit(solution)/shard_map/all_to_all | solution.py:55
  35.9 21.7 %all-gather.12.cloned.1.call-done = bf16[8,20,12416]{2,1,0:T(8,128)(2,1)} async-done(((bf16[1,20,12416]{2,1,0:T(8,128)(2,1)}), bf16[8,20,12416]{2,1,0:T(8,128)(2,1)}) %all-gather.12.cloned.1.call-update) | async-done | bytes 3973136 | tf_op jit(solution)/shard_map/all_gather | solution.py:47
  57.6 4.9 %fusion.8 = f32[8,20,512]{2,1,0:T(8,128)S(1)} fusion(bf16[6144,512]{1,0:T(8,128)(2,1)} %param.14, bf16[8,20,12416]{2,1,0:T(8,128)(2,1)} %all-gather.12.cloned.1.call-done), kind=kOutput, calls=%fused_computation.11 | convolution fusion | flops 1006632960 | bytes 8978432 | tf_op jit(solution)/shard_map/dot_general | solution.py:63
  62.5 0.1 reshape_reshape.10
  62.6 0.2 multiply_reduce_fusion.6
  63.0 5.0 %fusion.6 = f32[8,20,512]{2,1,0:T(8,128)S(1)} fusion(bf16[6144,512]{1,0:T(8,128)(2,1)} %param.15, bf16[8,20,12416]{2,1,0:T(8,128)(2,1)} %all-gather.12.cloned.1.call-done), kind=kOutput, calls=%fused_computation.9 | convolution fusion | flops 1006632960 | bytes 8978432 | tf_op jit(solution)/shard_map/dot_general | solution.py:63
  68.0 0.1 reshape_reshape.11
  68.1 0.2 multiply_reduce_fusion.5
  68.4 1.0 compare_reduce_fusion
  69.6 4.9 %fusion.29 = bf16[8,20,512]{2,1,0:T(8,128)(2,1)S(1)} fusion(bf16[6144,512]{1,0:T(8,128)(2,1)} %param.16, bf16[8,20,12416]{2,1,0:T(8,128)(2,1)} %all-gather.12.cloned.1.call-done), kind=kOutput, calls=%fused_computation.41 | convolution fusion | flops 1006714880 | bytes 8814592 | tf_op jit(solution)/shard_map/dot_general | solution.py:63
  74.7 0.4 fusion.63
  75.1 0.3 fusion.39
  75.5 1.5 collective-permute-start
  76.9 2.4 %collective-permute-start.2 = (bf16[160,512]{1,0:T(8,128)(2,1)S(1)}, bf16[160,512]{1,0:T(8,128)(2,1)}, u32[]{:S(2)}, u32[]{:S(2)}) collective-permute-start(bf16[160,512]{1,0:T(8,128)(2,1)S(1)} %bitcast.132), channel_id=1, source_target_pairs={{0,24},{8,0},{16,8},{24,16},{1,25},{9,1},{17,9},{25,17},{2,26},{10... | collective-permute-start | bytes 491528 | tf_op jit(solution)/shard_map/ppermute | solution.py:143
  79.3 0.5 collective-permute-start.1
  79.9 6.3 %fusion.34 = bf16[8,20,512]{2,1,0:T(8,128)(2,1)S(1)} fusion(bf16[512,6144]{1,0:T(8,128)(2,1)} %param.17, bf16[8,20,12416]{2,1,0:T(8,128)(2,1)} %all-gather.12.cloned.1.call-done), kind=kOutput, calls=%fused_computation.42 | convolution fusion | flops 1006714880 | bytes 8814592 | tf_op jit(solution)/shard_map/dot_general | solution.py:85
  86.3 0.2 fusion.40
  86.5 0.3 fusion.76
  86.8 0.5 multiply_reduce_fusion.3
  87.3 0.7 multiply_reduce_fusion.4
  88.0 0.2 copy_bitcast_fusion.2
  88.3 0.2 copy_bitcast_fusion.3
  88.6 5.7 %convolution_convert_fusion.1 = bf16[8,20,6144]{2,1,0:T(8,128)(2,1)} fusion(bf16[8,20,512]{2,1,0:T(8,128)(2,1)S(1)} %reshape.193, bf16[512,6144]{1,0:T(8,128)(2,1)} %param.17), kind=kOutput, calls=%fused_computation.2 | convolution fusion | flops 1007616000 | bytes 8421376 | tf_op jit(solution)/shard_map/dot_general | solution.py:107
  94.3 4.4 %all-to-all-start = ((bf16[8,20,6144]{2,1,0:T(8,128)(2,1)}), bf16[8,20,6144]{2,1,0:T(8,128)(2,1)}, u32[]{:S(2)}, u32[]{:S(2)}) async-start(bf16[8,20,6144]{2,1,0:T(8,128)(2,1)} %convolution_convert_fusion.1), calls=%async_computation | async-start | bytes 4718592 | tf_op jit(solution)/shard_map/all_to_all | solution.py:113
  98.7 0.2 all-gather.10.cloned.1.call-start
  98.9 0.8 pad_maximum_fusion.1
  99.8 4.3 %copy.144 = bf16[8,160,1536]{2,0,1:T(8,128)(2,1)S(1)} copy(bf16[8,160,1536]{2,1,0:T(8,128)(2,1)} %all-gather.8.cloned.1.call-done) | data formatting | bytes 7864320 | tf_op jit(solution)/shard_map/all_gather | solution.py:56
  104.0 0.3 slice_bitcast_fusion
  104.3 1.5 copy.146
  105.8 5.0 %constant_dynamic-slice_fusion.1 = (bf16[1,160,1536]{2,0,1:T(2,128)(2,1)}, bf16[1,160,1536]{2,0,1:T(2,128)(2,1)}, bf16[1,160,1536]{2,0,1:T(2,128)(2,1)S(1)}, bf16[1,160,1536]{2,0,1:T(2,128)(2,1)S(1)}) fusion(bf16[4,160,1536]{2,0,1:T(4,128)(2,1)S(1)} %bitcast.126, s32[]{:T(128)S(6)} %select_n.48, s32[]{:T(128)S(6)} %select_n.50, s32[]{:T(128)S(6)} %select_n.46, ...), kind=kLoop, calls=%fused_computation.130 | loop fusion | bytes 3932176 | tf_op jit(solution)/shard_map/jit(dynamic_index_in_dim)/dynamic_slice | solution.py:147
  110.9 0.6 fusion.59
  111.5 0.7 copy-done.7
  112.2 1.5 convolution_add_fusion.2
  113.7 2.0 %copy.145 = bf16[4,8,20,1536]{3,2,1,0:T(8,128)(2,1)} copy(bf16[4,8,20,1536]{3,1,2,0:T(8,128)(2,1)S(1)} %get-tuple-element.32) | data formatting | bytes 3932160 | tf_op jit(solution)/shard_map/transpose | solution.py:59
  115.7 4.0 %reshape.195 = bf16[640,1536]{1,0:T(8,128)(2,1)} reshape(bf16[4,8,20,1536]{3,2,1,0:T(8,128)(2,1)} %copy.145) | data formatting | bytes 3932160 | tf_op jit(solution)/shard_map/reshape | solution.py:59
  119.7 2.0 %fusion.52 = f32[512,1536]{1,0:T(8,128)S(1)} fusion(bf16[160,512]{1,0:T(8,128)(2,1)} %collective-permute-done.2, bf16[1,160,1536]{2,0,1:T(2,128)(2,1)} %get-tuple-element.34), kind=kOutput, calls=%fused_computation.65 | convolution fusion | flops 251658240 | bytes 3801088 | tf_op jit(solution)/shard_map/dot_general | solution.py:145
  121.7 1.8 %fusion.13 = bf16[512,1536]{1,0:T(8,128)(2,1)} fusion(f32[512,1536]{1,0:T(8,128)S(1)} %fusion.52, f32[512,1536]{1,0:T(8,128)S(1)} %convolution_add_fusion.2, bf16[160,512]{1,0:T(8,128)(2,1)S(1)} %collective-permute-done.1, bf16[1,160,1536]{2,0,1:T(2,128)(2,1)S(1)} %copy-done.6), kind=kOutput, calls=%fused_computation.19 | convolution fusion | flops 254017536 | bytes 8519680 | tf_op jit(solution)/shard_map/dot_general | solution.py:145
  123.5 4.6 %all-to-all-done = bf16[8,20,6144]{2,1,0:T(8,128)(2,1)} async-done(((bf16[8,20,6144]{2,1,0:T(8,128)(2,1)}), bf16[8,20,6144]{2,1,0:T(8,128)(2,1)}, u32[]{:S(2)}, u32[]{:S(2)}) %all-to-all-start) | async-done | bytes 1966112 | tf_op jit(solution)/shard_map/all_to_all | solution.py:113
  128.1 2.1 %convert_reduce_fusion = f32[20,6144]{1,0:T(8,128)S(1)} fusion(bf16[8,20,6144]{2,1,0:T(8,128)(2,1)} %all-to-all-done), kind=kLoop, calls=%fused_computation.15 | loop fusion | flops 1843200 | bytes 2457600 | tf_op jit(solution)/shard_map/reduce_sum | solution.py:114
  130.2 0.2 multiply_reduce_fusion.1
  130.4 0.4 fusion.98
  130.8 8.3 %all-gather.2 = f32[49152]{0:T(1024)S(1)} all-gather(f32[6144]{0:T(1024)S(1)} %bitcast.136), channel_id=4, replica_groups=mesh['dp'=4,'ctx'=8] {'ctx'}, dimensions={0}, use_global_device_ids=true | all-gather | bytes 221184 | tf_op jit(solution)/shard_map/all_gather | solution.py:120
  139.2 1.5 collective-permute-start.3
  140.8 1.0 collective-permute-start.4
  141.7 2.8 %collective-permute-start.5 = (f32[6144]{0:T(1024)S(1)}, f32[6144]{0:T(1024)S(1)}, u32[]{:S(2)}, u32[]{:S(2)}) collective-permute-start(f32[6144]{0:T(1024)S(1)} %reduce_sum.108), channel_id=1, source_target_pairs={{0,24},{8,0},{16,8},{24,16},{1,25},{9,1},{17,9},{25,17},{2,26},{10... | collective-permute-start | bytes 73736 | tf_op jit(solution)/shard_map/ppermute | solution.py:156
  144.6 2.8 %fusion.2 = bf16[1,128,6144]{2,1,0:T(8,128)(2,1)} fusion(bf16[1,128,6144]{2,1,0:T(8,128)(2,1)S(1)} %copy-done.4, f32[20,6144]{1,0:T(8,128)S(1)} %convert_reduce_fusion, f32[20]{0:T(128)S(1)} %fusion.44, s32[20]{0:T(128)S(1)} %bitcast.144, pred[20]{0:T(512)(128)(4,1)S(1)} %get-tuple-element.26), kind=kOutput, calls=%fused_computation.5 | convolution fusion | flops 191230976 | bytes 3637428 | tf_op jit(solution)/shard_map/dot_general | solution.py:116
  147.4 0.4 dynamic_update_slice.13
  147.8 0.4 dynamic_update_slice.14
  148.2 0.4 dynamic_update_slice.15
  148.5 0.4 dynamic_update_slice.16
  148.9 0.7 reduce_sum.109
  149.6 6.1 %convolution_convert_fusion = bf16[1536,1536]{1,0:T(8,128)(2,1)S(1)} fusion(bf16[640,1536]{1,0:T(8,128)(2,1)} %reshape.195, bf16[640,1536]{1,0:T(8,128)(2,1)} %all-gather.10.cloned.1.call-done), kind=kOutput, calls=%fused_computation.1 | convolution fusion | flops 3022258176 | bytes 8650752 | tf_op jit(solution)/shard_map/dot_general | solution.py:126
  155.7 2.3 %fusion.109 = (bf16[1536,512]{1,0:T(8,128)(2,1)}, bf16[1536,512]{1,0:T(8,128)(2,1)}, bf16[1536,512]{1,0:T(8,128)(2,1)}) fusion(bf16[1536,1536]{1,0:T(8,128)(2,1)S(1)} %convolution_convert_fusion), kind=kLoop, calls=%fused_computation.146 | loop fusion | bytes 9437184 | tf_op jit(solution)/shard_map/slice | solution.py:133
  (46 shorter events, 0.9 us)
Async XLA Ops:
  7.2 5.8 %copy-start = (bf16[1,128,6144]{2,1,0:T(8,128)(2,1)S(1)}, bf16[1,128,6144]{2,1,0:T(8,128)(2,1)}, u32[]{:S(2)}) copy-start(bf16[1,128,6144]{2,1,0:T(8,128)(2,1)} %param.12) | copy-start | bytes 4718596
  7.2 50.4 %all-gather.12.cloned.1.call-start = ((), (), s32[]{:S(2)}) async-start(), calls=%async_computation.4 | async-start | bytes 5363712 | tf_op jit(solution)/shard_map/all_gather | solution.py:47
  11.1 1.5 copy-start.2
  15.7 84.1 %all-gather.8.cloned.1.call-start = ((), (), s32[]{:S(2)}) async-start(), calls=%async_computation.2 | async-start | bytes 4423680 | tf_op jit(solution)/shard_map/all_gather | solution.py:56
  75.5 36.0 %collective-permute-start = (bf16[160,512]{1,0:T(8,128)(2,1)S(1)}, bf16[160,512]{1,0:T(8,128)(2,1)S(1)}, u32[]{:S(2)}, u32[]{:S(2)}) collective-permute-start(bf16[160,512]{1,0:T(8,128)(2,1)S(1)} %bitcast.131), channel_id=1, source_target_pairs={{0,8},{8,16},{16,24},{24,0},{1,9},{9,17},{17,25},{25,1},{2,10},{10... | collective-permute-start | bytes 491528 | tf_op jit(solution)/shard_map/ppermute | solution.py:143
  76.9 42.8 %collective-permute-start.2 = (bf16[160,512]{1,0:T(8,128)(2,1)S(1)}, bf16[160,512]{1,0:T(8,128)(2,1)}, u32[]{:S(2)}, u32[]{:S(2)}) collective-permute-start(bf16[160,512]{1,0:T(8,128)(2,1)S(1)} %bitcast.132), channel_id=1, source_target_pairs={{0,24},{8,0},{16,8},{24,16},{1,25},{9,1},{17,9},{25,17},{2,26},{10... | collective-permute-start | bytes 491528 | tf_op jit(solution)/shard_map/ppermute | solution.py:143
  79.3 42.4 %collective-permute-start.1 = (bf16[160,512]{1,0:T(8,128)(2,1)S(1)}, bf16[160,512]{1,0:T(8,128)(2,1)S(1)}, u32[]{:S(2)}, u32[]{:S(2)}) collective-permute-start(bf16[160,512]{1,0:T(8,128)(2,1)S(1)} %bitcast.133), channel_id=1, source_target_pairs={{0,16},{8,24},{16,0},{24,8},{1,17},{9,25},{17,1},{25,9},{2,18},{10... | collective-permute-start | bytes 491528 | tf_op jit(solution)/shard_map/ppermute | solution.py:143
  94.3 33.8 %all-to-all-start = ((bf16[8,20,6144]{2,1,0:T(8,128)(2,1)}), bf16[8,20,6144]{2,1,0:T(8,128)(2,1)}, u32[]{:S(2)}, u32[]{:S(2)}) async-start(bf16[8,20,6144]{2,1,0:T(8,128)(2,1)} %convolution_convert_fusion.1), calls=%async_computation | async-start | bytes 4718592 | tf_op jit(solution)/shard_map/all_to_all | solution.py:113
  98.7 50.9 %all-gather.10.cloned.1.call-start = ((), (), s32[]{:S(2)}) async-start(), calls=%async_computation.3 | async-start | bytes 2457600 | tf_op jit(solution)/shard_map/all_gather | solution.py:121
  111.5 0.7 copy-start.7
  119.7 2.0 %copy-start.6 = (bf16[1,160,1536]{2,0,1:T(2,128)(2,1)S(1)}, bf16[1,160,1536]{2,0,1:T(2,128)(2,1)}, u32[]{:S(2)}) copy-start(bf16[1,160,1536]{2,0,1:T(2,128)(2,1)} %get-tuple-element.33) | copy-start | bytes 1474564
  123.5 6.7 %copy-start.5 = (f32[20,6144]{1,0:T(8,128)S(1)}, f32[20,6144]{1,0:T(8,128)}, u32[]{:S(2)}) copy-start(f32[20,6144]{1,0:T(8,128)} %get-tuple-element.40) | copy-start | bytes 1474564
  123.5 6.9 %copy-start.3 = (f32[20,6144]{1,0:T(8,128)S(1)}, f32[20,6144]{1,0:T(8,128)}, u32[]{:S(2)}) copy-start(f32[20,6144]{1,0:T(8,128)} %copy-done.2) | copy-start | bytes 1474564
  123.5 21.1 %copy-start.4 = (bf16[1,128,6144]{2,1,0:T(8,128)(2,1)S(1)}, bf16[1,128,6144]{2,1,0:T(8,128)(2,1)}, u32[]{:S(2)}) copy-start(bf16[1,128,6144]{2,1,0:T(8,128)(2,1)} %param.11) | copy-start | bytes 4718596
  139.2 8.5 %collective-permute-start.3 = (f32[6144]{0:T(1024)S(1)}, f32[6144]{0:T(1024)S(1)}, u32[]{:S(2)}, u32[]{:S(2)}) collective-permute-start(f32[6144]{0:T(1024)S(1)} %reduce_sum.108), channel_id=1, source_target_pairs={{0,8},{8,16},{16,24},{24,0},{1,9},{9,17},{17,25},{25,1},{2,10},{10... | collective-permute-start | bytes 73736 | tf_op jit(solution)/shard_map/ppermute | solution.py:156
  140.8 7.4 %collective-permute-start.4 = (f32[6144]{0:T(1024)S(1)}, f32[6144]{0:T(1024)S(1)}, u32[]{:S(2)}, u32[]{:S(2)}) collective-permute-start(f32[6144]{0:T(1024)S(1)} %reduce_sum.108), channel_id=1, source_target_pairs={{0,16},{8,24},{16,0},{24,8},{1,17},{9,25},{17,1},{25,9},{2,18},{10... | collective-permute-start | bytes 73736 | tf_op jit(solution)/shard_map/ppermute | solution.py:156
  141.7 6.8 %collective-permute-start.5 = (f32[6144]{0:T(1024)S(1)}, f32[6144]{0:T(1024)S(1)}, u32[]{:S(2)}, u32[]{:S(2)}) collective-permute-start(f32[6144]{0:T(1024)S(1)} %reduce_sum.108), channel_id=1, source_target_pairs={{0,24},{8,0},{16,8},{24,16},{1,25},{9,1},{17,9},{25,17},{2,26},{10... | collective-permute-start | bytes 73736 | tf_op jit(solution)/shard_map/ppermute | solution.py:156
  149.6 8.4 %copy-start.1 = (bf16[1,128,6144]{2,1,0:T(8,128)(2,1)S(1)}, bf16[1,128,6144]{2,1,0:T(8,128)(2,1)}, u32[]{:S(2)}) copy-start(bf16[1,128,6144]{2,1,0:T(8,128)(2,1)} %param.12) | copy-start | bytes 4718596
Sparse Core Ops, SparseCore 0:
  15.8 41.8 all-gather.11
  59.5 35.6 all-gather.7
  101.1 45.1 all-gather.9
where the time goes:
time: 165 us
  matrix products  49 us (30%)
  blocking collectives  28.3 us (17%)
  waiting for transfers between devices  26.4 us (16%)
  local copies, waits for them, and re-layouts  22.6 us (14%)
  between operations  14.8 us (9%)
  starting transfers between devices  14.4 us (9%)
  other arithmetic  8.98 us (5%)
    all_gather x1, waiting for transfers between devices, body(): lax.all_gather(jnp.concatenate([normed, delta, flag_cols], axis=1), 'ctx'...  21.7 us
    all_to_all x1, blocking collectives, body(): lax.all_to_all(jnp.concatenate([normed, delta], axis=0), 'dp', 1, 0, tile...  20 us
    dot_general x3, matrix products, project(): lax.dot_general(chunk_normed, weight, (((2,), (0,)), ((), ())), preferred...  14.8 us
    all_gather x1, blocking collectives, body(): lax.all_gather(router_part, 'ctx', axis=0, tiled=False)  8.3 us
    dot_general x1, matrix products, body(): lax.dot_general(chunk_delta, w_out, (((2,), (1,)), ((), ())), preferred_e...  6.33 us
    dot_general x1, matrix products, contract(): lax.dot_general(left, right, (((0,), (0,)), ((), ())), preferred_element_...  6.13 us
    dot_general x1, matrix products, body(): lax.dot_general(mixed_late.reshape(n_ctx, capacity, inner), w_out, (((2,)...  5.71 us
    ppermute x3, starting transfers between devices, body(): lax.ppermute(router_group, 'dp', [(i, (i + shift) % n_dp) for i in range(...  5.36 us
  transfers between devices with their start and end apart: 10, of which 2 were waited for; matrix products, arithmetic and copies ran while one was open for 39% of the time, Pallas kernels for 0%

commit v1 on v0

--- a/solution.py
+++ b/solution.py
@@ -52,7 +52,16 @@
     all_present = packed[:, :, 2 * width].reshape(n_ctx * capacity)
     slots = n_ctx * capacity
     block = width // n_dp
-    own_blocks = lax.all_to_all(jnp.concatenate([normed, delta], axis=0), "dp", 1, 0, tiled=True)
+    x = jnp.concatenate([normed, delta], axis=0)
+    ways, here = (lax.axis_size("dp"), lax.axis_index("dp"))
+    width_2 = x.shape[1] // ways
+    turned = jnp.roll(x, -here * width_2, axis=1)
+    got = [lax.slice_in_dim(turned, 0, width_2, axis=1)]
+    for far in range(1, ways):
+        sent = lax.slice_in_dim(turned, far * width_2, (far + 1) * width_2, axis=1)
+        got.append(lax.ppermute(sent, "dp", [(d, (d + far) % ways) for d in range(ways)]))
+    line = jnp.concatenate(got[::-1], axis=0)
+    own_blocks = jnp.roll(line, (here + 1) * got[0].shape[0], axis=0)
     pieces = lax.all_gather(own_blocks, "ctx", axis=0, tiled=False).reshape(
         n_ctx, n_dp, 2, capacity, block
     )

time: 165 us -> 168 us (1.018)
  blocking collectives: 28.3 us -> 8.43 us
  waiting for transfers between devices: 26.4 us -> 36.4 us
  local copies, waits for them, and re-layouts: 22.6 us -> 28.8 us
  starting transfers between devices: 14.4 us -> 18.8 us
  other arithmetic: 8.98 us -> 10.7 us
    all_to_all x1 -> x0, blocking collectives: 20 us -> none  [body(): lax.all_to_all(jnp.concatenate([normed, delta], axis=0), 'dp', 1, 0, tile...]
    ppermute x0 -> x3, waiting for transfers between devices: none -> 9.93 us  [body(): lax.ppermute(sent, 'dp', [(d, (d + far) % ways) for d in range(ways)])]
    reshape x0 -> x1, local copies, waits for them, and re-layouts: none -> 6.82 us  [body(): lax.all_gather(own_blocks, 'ctx', axis=0, tiled=False)]
    ppermute x0 -> x3, starting transfers between devices: none -> 6.11 us  [body(): lax.ppermute(sent, 'dp', [(d, (d + far) % ways) for d in range(ways)])]
    all_gather x1 -> x0, local copies, waits for them, and re-layouts: 4.27 us -> none  [body(): lax.all_gather(own_blocks, 'ctx', axis=0, tiled=False)]
    ppermute x3, starting transfers between devices: 5.36 us -> 2.08 us  [body(): lax.ppermute(router_group, 'dp', [(i, (i + shift) % n_dp) for i in range(...]
    all_to_all x1, waiting for transfers between devices: 4.57 us -> 1.47 us  [body(): received = lax.all_to_all(contributions, 'ctx', 0, 0, tiled=True)]
    transpose x2, local copies, waits for them, and re-layouts: 1.77 us -> 4.16 us  [body(): pieces[:, :, 1].transpose(1, 0, 2, 3).reshape(n_dp * slots, block)]
  transfers between devices with their start and end apart: 10 -> 13, of which waited for: 2 -> 5; matrix products, arithmetic and copies ran while one was open for 39% -> 43% of each run, Pallas kernels for 0% -> 0%
where the time goes in v1:
time: 168 us; the launch traced here: 167 us
  matrix products  48.9 us (29%)
  waiting for transfers between devices  36.4 us (22%)
  local copies, waits for them, and re-layouts  28.8 us (17%)
  starting transfers between devices  18.8 us (11%)
  between operations  14.9 us (9%)
  other arithmetic  10.7 us (6%)
  blocking collectives  8.43 us (5%)
    all_gather x1, waiting for transfers between devices, body(): lax.all_gather(jnp.concatenate([normed, delta, flag_cols], axis=1), 'ctx'...  22.9 us
    dot_general x3, matrix products, project(): lax.dot_general(chunk_normed, weight, (((2,), (0,)), ((), ())), preferred...  14.9 us
    ppermute x3, waiting for transfers between devices, body(): lax.ppermute(sent, 'dp', [(d, (d + far) % ways) for d in range(ways)])  9.93 us
    all_gather x1, blocking collectives, body(): lax.all_gather(router_part, 'ctx', axis=0, tiled=False)  8.43 us
    reshape x1, local copies, waits for them, and re-layouts, body(): lax.all_gather(own_blocks, 'ctx', axis=0, tiled=False)  6.82 us
    ppermute x3, starting transfers between devices, body(): lax.ppermute(mixed, 'dp', [(i, (i + shift) % n_dp) for i in range(n_dp)])  6.15 us
    dot_general x1, matrix products, contract(): lax.dot_general(left, right, (((0,), (0,)), ((), ())), preferred_element_...  6.13 us
    ppermute x3, starting transfers between devices, body(): lax.ppermute(sent, 'dp', [(d, (d + far) % ways) for d in range(ways)])  6.11 us
  transfers between devices with their start and end apart: 13, of which 5 were waited for; matrix products, arithmetic and copies ran while one was open for 43% of the time, Pallas kernels for 0%

profile of v1, /device:TPU:0, one launch (start us, length us, event | category | flops | bytes accessed | tf_op | source)
XLA Modules:
  0.0 167.0 jit_solution(426771288786683549)
XLA Ops:
  7.2 0.6 compare_reduce_fusion.1
  8.5 0.7 compare_and_fusion
  9.4 1.9 %multiply_reduce_fusion.2 = (f32[20]{0:T(128)S(1)}, f32[20,6144]{1,0:T(8,128)S(1)}) fusion(bf16[1,128,6144]{2,1,0:T(8,128)(2,1)} %param.11, s32[20]{0:T(128)S(1)} %bitcast.126, pred[20]{0:T(512)(128)(4,1)S(1)} %get-tuple-element.26), kind=kOutput, calls=%fused_computation.65 | convolution fusion | flops 31708140 | bytes 2064564 | tf_op jit(solution)/shard_map/dot_general | solution.py:38
  11.3 1.4 fusion.44
  12.9 1.2 multiply_convert_fusion
  14.1 0.7 fusion.94
  14.8 0.9 fusion.50
  15.7 1.8 %fusion.53 = bf16[40,6144]{1,0:T(8,128)(2,1)S(1)} fusion(s32[]{:T(128)S(6)} %select_n.67, bf16[20,6144]{1,0:T(8,128)(2,1)S(1)} %multiply_convert_fusion.1, bf16[20,6144]{1,0:T(8,128)(2,1)S(1)} %get-tuple-element.42), kind=kLoop, calls=%fused_computation.67 | loop fusion | flops 1966080 | bytes 983044 | tf_op jit(solution)/shard_map/jit(_roll_dynamic)/concatenate | solution.py:58
  17.6 5.1 %collective-permute-start = (bf16[40,1536]{1,0:T(8,128)(2,1)S(1)}, bf16[40,1536]{1,0:T(8,128)(2,1)S(1)}, u32[]{:S(2)}, u32[]{:S(2)}) collective-permute-start(bf16[40,1536]{1,0:T(8,128)(2,1)S(1)} %get-tuple-element.39), channel_id=1, source_target_pairs={{0,24},{8,0},{16,8},{24,16},{1,25},{9,1},{17,9},{25,17},{2,26},{10... | collective-permute-start | bytes 368648 | tf_op jit(solution)/shard_map/ppermute | solution.py:62
  22.7 1.0 collective-permute-start.1
  23.7 2.7 %collective-permute-done = bf16[40,1536]{1,0:T(8,128)(2,1)S(1)} collective-permute-done((bf16[40,1536]{1,0:T(8,128)(2,1)S(1)}, bf16[40,1536]{1,0:T(8,128)(2,1)S(1)}, u32[]{:S(2)}, u32[]{:S(2)}) %collective-permute-start) | collective-permute-done | bytes 122912 | tf_op jit(solution)/shard_map/ppermute | solution.py:62
  26.5 7.2 %collective-permute-done.1 = bf16[40,1536]{1,0:T(8,128)(2,1)S(1)} collective-permute-done((bf16[40,1536]{1,0:T(8,128)(2,1)S(1)}, bf16[40,1536]{1,0:T(8,128)(2,1)S(1)}, u32[]{:S(2)}, u32[]{:S(2)}) %collective-permute-start.1) | collective-permute-done | bytes 122912 | tf_op jit(solution)/shard_map/ppermute | solution.py:62
  33.8 0.9 constant_dynamic-slice_fusion.4
  34.8 22.9 %all-gather.13.cloned.1.call-done = bf16[8,20,12416]{2,1,0:T(8,128)(2,1)} async-done(((bf16[1,20,12416]{2,1,0:T(8,128)(2,1)}), bf16[8,20,12416]{2,1,0:T(8,128)(2,1)}) %all-gather.13.cloned.1.call-update) | async-done | bytes 3973136 | tf_op jit(solution)/shard_map/all_gather | solution.py:47
  57.6 1.0 compare_reduce_fusion
  58.7 4.9 %fusion.29 = bf16[8,20,512]{2,1,0:T(8,128)(2,1)S(1)} fusion(bf16[6144,512]{1,0:T(8,128)(2,1)} %param.16, bf16[8,20,12416]{2,1,0:T(8,128)(2,1)} %all-gather.13.cloned.1.call-done), kind=kOutput, calls=%fused_computation.41 | convolution fusion | flops 1006714880 | bytes 8814592 | tf_op jit(solution)/shard_map/dot_general | solution.py:72
  63.7 5.0 %fusion.6 = f32[8,20,512]{2,1,0:T(8,128)S(1)} fusion(bf16[6144,512]{1,0:T(8,128)(2,1)} %param.15, bf16[8,20,12416]{2,1,0:T(8,128)(2,1)} %all-gather.13.cloned.1.call-done), kind=kOutput, calls=%fused_computation.9 | convolution fusion | flops 1006632960 | bytes 8978432 | tf_op jit(solution)/shard_map/dot_general | solution.py:72
  68.9 4.9 %fusion.8 = f32[8,20,512]{2,1,0:T(8,128)S(1)} fusion(bf16[6144,512]{1,0:T(8,128)(2,1)} %param.14, bf16[8,20,12416]{2,1,0:T(8,128)(2,1)} %all-gather.13.cloned.1.call-done), kind=kOutput, calls=%fused_computation.11 | convolution fusion | flops 1006632960 | bytes 8978432 | tf_op jit(solution)/shard_map/dot_general | solution.py:72
  73.9 0.2 multiply_reduce_fusion.6
  74.2 0.2 multiply_reduce_fusion.5
  74.7 0.4 fusion.66
  75.1 0.3 fusion.39
  75.5 0.7 copy-done.6
  76.1 0.7 copy.207
  76.8 2.3 %collective-permute-start.4 = (bf16[160,512]{1,0:T(8,128)(2,1)}, bf16[160,512]{1,0:T(8,128)(2,1)}, u32[]{:S(2)}, u32[]{:S(2)}) collective-permute-start(bf16[160,512]{1,0:T(8,128)(2,1)} %bitcast.115), channel_id=1, source_target_pairs={{0,16},{8,24},{16,0},{24,8},{1,17},{9,25},{17,1},{25,9},{2,18},{10... | collective-permute-start | bytes 491528 | tf_op jit(solution)/shard_map/ppermute | solution.py:152
  79.2 1.5 collective-permute-start.3
  80.6 2.3 %collective-permute-start.5 = (bf16[160,512]{1,0:T(8,128)(2,1)}, bf16[160,512]{1,0:T(8,128)(2,1)}, u32[]{:S(2)}, u32[]{:S(2)}) collective-permute-start(bf16[160,512]{1,0:T(8,128)(2,1)} %bitcast.115), channel_id=1, source_target_pairs={{0,24},{8,0},{16,8},{24,16},{1,25},{9,1},{17,9},{25,17},{2,26},{10... | collective-permute-start | bytes 491528 | tf_op jit(solution)/shard_map/ppermute | solution.py:152
  83.0 5.7 %fusion.34 = bf16[8,20,512]{2,1,0:T(8,128)(2,1)S(1)} fusion(bf16[512,6144]{1,0:T(8,128)(2,1)} %param.17, bf16[8,20,12416]{2,1,0:T(8,128)(2,1)} %all-gather.13.cloned.1.call-done), kind=kOutput, calls=%fused_computation.42 | convolution fusion | flops 1006714880 | bytes 8814592 | tf_op jit(solution)/shard_map/dot_general | solution.py:94
  88.8 0.2 fusion.40
  89.0 0.3 fusion.79
  89.3 0.5 multiply_reduce_fusion.3
  89.8 0.7 multiply_reduce_fusion.4
  90.5 0.2 copy_bitcast_fusion.1
  90.8 0.2 copy_bitcast_fusion.2
  91.0 1.0 reshape.189
  92.0 5.7 %convolution_convert_fusion.1 = bf16[8,20,6144]{2,1,0:T(8,128)(2,1)} fusion(bf16[8,20,512]{2,1,0:T(8,128)(2,1)S(1)} %reshape.189, bf16[512,6144]{1,0:T(8,128)(2,1)} %param.17), kind=kOutput, calls=%fused_computation.2 | convolution fusion | flops 1007616000 | bytes 8421376 | tf_op jit(solution)/shard_map/dot_general | solution.py:116
  97.7 4.4 %all-to-all-start = ((bf16[8,20,6144]{2,1,0:T(8,128)(2,1)}), bf16[8,20,6144]{2,1,0:T(8,128)(2,1)}, u32[]{:S(2)}, u32[]{:S(2)}) async-start(bf16[8,20,6144]{2,1,0:T(8,128)(2,1)} %convolution_convert_fusion.1), calls=%async_computation | async-start | bytes 4718592 | tf_op jit(solution)/shard_map/all_to_all | solution.py:122
  102.1 0.8 pad_maximum_fusion
  103.0 6.8 %reshape.190 = bf16[8,4,2,20,1536]{4,3,2,1,0:T(8,128)(2,1)} reshape(bf16[1280,1536]{1,0:T(8,128)(2,1)} %all-gather.9.cloned.1.call-done) | data formatting | bytes 7864320 | tf_op jit(solution)/shard_map/reshape | solution.py:65
  109.8 3.1 %slice_bitcast_fusion = (bf16[4,8,20,1536]{3,2,0,1:T(8,128)(2,1)S(1)}, bf16[4,8,20,1536]{3,2,0,1:T(8,128)(2,1)S(1)}) fusion(bf16[8,4,2,20,1536]{4,3,2,1,0:T(8,128)(2,1)} %reshape.190), kind=kLoop, calls=%fused_computation.20 | loop fusion | bytes 7864320 | tf_op jit(solution)/shard_map/transpose | solution.py:69
  113.0 1.0 copy.134
  114.0 1.6 copy.133
  115.6 4.0 %reshape.191 = bf16[640,1536]{1,0:T(8,128)(2,1)} reshape(bf16[4,8,20,1536]{3,2,1,0:T(8,128)(2,1)} %copy.133) | data formatting | bytes 3932160 | tf_op jit(solution)/shard_map/reshape | solution.py:68
  119.5 4.1 %constant_dynamic-slice_fusion.1 = (bf16[1,160,1536]{2,0,1:T(2,128)(2,1)S(1)}, bf16[1,160,1536]{2,0,1:T(2,128)(2,1)S(1)}, bf16[1,160,1536]{2,0,1:T(2,128)(2,1)S(1)}, bf16[1,160,1536]{2,0,1:T(2,128)(2,1)S(1)}) fusion(bf16[4,160,1536]{2,0,1:T(4,128)(2,1)S(1)} %bitcast.118, s32[]{:T(128)S(6)} %select_n.74, s32[]{:T(128)S(6)} %select_n.76, s32[]{:T(128)S(6)} %select_n.72, ...), kind=kLoop, calls=%fused_computation.137 | loop fusion | bytes 3932176 | tf_op jit(solution)/shard_map/jit(dynamic_index_in_dim)/dynamic_slice | solution.py:156
  123.6 0.6 fusion.62
  124.3 1.5 convolution_add_fusion.2
  125.8 1.5 fusion.55
  127.4 2.7 %fusion.13 = bf16[512,1536]{1,0:T(8,128)(2,1)} fusion(f32[512,1536]{1,0:T(8,128)S(1)} %fusion.55, f32[512,1536]{1,0:T(8,128)S(1)} %convolution_add_fusion.2, bf16[160,512]{1,0:T(8,128)(2,1)} %collective-permute-done.4, bf16[1,160,1536]{2,0,1:T(2,128)(2,1)S(1)} %get-tuple-element.33), kind=kOutput, calls=%fused_computation.19 | convolution fusion | flops 254017536 | bytes 8519680 | tf_op jit(solution)/shard_map/dot_general | solution.py:154
  130.0 1.5 all-to-all-done
  131.5 2.1 %convert_reduce_fusion = f32[20,6144]{1,0:T(8,128)S(1)} fusion(bf16[8,20,6144]{2,1,0:T(8,128)(2,1)} %all-to-all-done), kind=kLoop, calls=%fused_computation.15 | loop fusion | flops 1843200 | bytes 2457600 | tf_op jit(solution)/shard_map/reduce_sum | solution.py:123
  133.8 0.4 fusion.101
  134.2 8.4 %all-gather.3 = f32[49152]{0:T(1024)S(1)} all-gather(f32[6144]{0:T(1024)S(1)} %bitcast.120), channel_id=5, replica_groups=mesh['dp'=4,'ctx'=8] {'ctx'}, dimensions={0}, use_global_device_ids=true | all-gather | bytes 221184 | tf_op jit(solution)/shard_map/all_gather | solution.py:129
  142.8 0.8 collective-permute-start.8
  143.5 0.9 collective-permute-start.7
  144.4 0.4 collective-permute-start.6
  144.9 2.8 %fusion.2 = bf16[1,128,6144]{2,1,0:T(8,128)(2,1)} fusion(bf16[1,128,6144]{2,1,0:T(8,128)(2,1)S(1)} %copy-done.4, f32[20,6144]{1,0:T(8,128)S(1)} %convert_reduce_fusion, f32[20]{0:T(128)S(1)} %fusion.44, s32[20]{0:T(128)S(1)} %bitcast.128, pred[20]{0:T(512)(128)(4,1)S(1)} %get-tuple-element.26), kind=kOutput, calls=%fused_computation.5 | convolution fusion | flops 191230976 | bytes 3637428 | tf_op jit(solution)/shard_map/dot_general | solution.py:125
  147.6 0.4 dynamic_update_slice.13
  148.0 2.0 %collective-permute-done.6 = f32[6144]{0:T(1024)S(1)} collective-permute-done((f32[6144]{0:T(1024)S(1)}, f32[6144]{0:T(1024)S(1)}, u32[]{:S(2)}, u32[]{:S(2)}) %collective-permute-start.6) | collective-permute-done | bytes 24608 | tf_op jit(solution)/shard_map/ppermute | solution.py:165
  150.1 0.3 dynamic_update_slice.14
  150.4 0.4 dynamic_update_slice.15
  150.8 0.6 dynamic_update_slice.16
  151.4 0.7 reduce_sum.109
  152.1 6.1 %convolution_convert_fusion = bf16[1536,1536]{1,0:T(8,128)(2,1)S(1)} fusion(bf16[640,1536]{1,0:T(8,128)(2,1)} %reshape.191, bf16[640,1536]{1,0:T(8,128)(2,1)} %all-gather.11.cloned.1.call-done), kind=kOutput, calls=%fused_computation.1 | convolution fusion | flops 3022258176 | bytes 8650752 | tf_op jit(solution)/shard_map/dot_general | solution.py:135
  158.2 2.3 %fusion.112 = (bf16[1536,512]{1,0:T(8,128)(2,1)}, bf16[1536,512]{1,0:T(8,128)(2,1)}, bf16[1536,512]{1,0:T(8,128)(2,1)}) fusion(bf16[1536,1536]{1,0:T(8,128)(2,1)S(1)} %convolution_convert_fusion), kind=kLoop, calls=%fused_computation.160 | loop fusion | bytes 9437184 | tf_op jit(solution)/shard_map/slice | solution.py:142
  (60 shorter events, 1.8 us)
Async XLA Ops:
  7.2 5.7 %copy-start = (bf16[1,128,6144]{2,1,0:T(8,128)(2,1)S(1)}, bf16[1,128,6144]{2,1,0:T(8,128)(2,1)}, u32[]{:S(2)}) copy-start(bf16[1,128,6144]{2,1,0:T(8,128)(2,1)} %param.12) | copy-start | bytes 4718596
  7.2 50.4 %all-gather.13.cloned.1.call-start = ((), (), s32[]{:S(2)}) async-start(), calls=%async_computation.3 | async-start | bytes 5363712 | tf_op jit(solution)/shard_map/all_gather | solution.py:47
  11.3 1.5 copy-start.2
  15.7 87.3 %all-gather.9.cloned.1.call-start = ((), (), s32[]{:S(2)}) async-start(), calls=%async_computation.1 | async-start | bytes 4423680 | tf_op jit(solution)/shard_map/all_gather | solution.py:65
  17.6 8.8 %collective-permute-start = (bf16[40,1536]{1,0:T(8,128)(2,1)S(1)}, bf16[40,1536]{1,0:T(8,128)(2,1)S(1)}, u32[]{:S(2)}, u32[]{:S(2)}) collective-permute-start(bf16[40,1536]{1,0:T(8,128)(2,1)S(1)} %get-tuple-element.39), channel_id=1, source_target_pairs={{0,24},{8,0},{16,8},{24,16},{1,25},{9,1},{17,9},{25,17},{2,26},{10... | collective-permute-start | bytes 368648 | tf_op jit(solution)/shard_map/ppermute | solution.py:62
  22.7 11.0 %collective-permute-start.2 = (bf16[40,1536]{1,0:T(8,128)(2,1)S(1)}, bf16[40,1536]{1,0:T(8,128)(2,1)S(1)}, u32[]{:S(2)}, u32[]{:S(2)}) collective-permute-start(bf16[40,1536]{1,0:T(8,128)(2,1)S(1)} %get-tuple-element.37), channel_id=1, source_target_pairs={{0,8},{8,16},{16,24},{24,0},{1,9},{9,17},{17,25},{25,1},{2,10},{10... | collective-permute-start | bytes 368648 | tf_op jit(solution)/shard_map/ppermute | solution.py:62
  22.7 10.9 %collective-permute-start.1 = (bf16[40,1536]{1,0:T(8,128)(2,1)S(1)}, bf16[40,1536]{1,0:T(8,128)(2,1)S(1)}, u32[]{:S(2)}, u32[]{:S(2)}) collective-permute-start(bf16[40,1536]{1,0:T(8,128)(2,1)S(1)} %get-tuple-element.38), channel_id=1, source_target_pairs={{0,16},{8,24},{16,0},{24,8},{1,17},{9,25},{17,1},{25,9},{2,18},{10... | collective-permute-start | bytes 368648 | tf_op jit(solution)/shard_map/ppermute | solution.py:62
  75.5 0.7 copy-start.6
  76.8 50.5 %collective-permute-start.4 = (bf16[160,512]{1,0:T(8,128)(2,1)}, bf16[160,512]{1,0:T(8,128)(2,1)}, u32[]{:S(2)}, u32[]{:S(2)}) collective-permute-start(bf16[160,512]{1,0:T(8,128)(2,1)} %bitcast.115), channel_id=1, source_target_pairs={{0,16},{8,24},{16,0},{24,8},{1,17},{9,25},{17,1},{25,9},{2,18},{10... | collective-permute-start | bytes 491528 | tf_op jit(solution)/shard_map/ppermute | solution.py:152
  79.2 45.1 %collective-permute-start.3 = (bf16[160,512]{1,0:T(8,128)(2,1)}, bf16[160,512]{1,0:T(8,128)(2,1)}, u32[]{:S(2)}, u32[]{:S(2)}) collective-permute-start(bf16[160,512]{1,0:T(8,128)(2,1)} %bitcast.115), channel_id=1, source_target_pairs={{0,8},{8,16},{16,24},{24,0},{1,9},{9,17},{17,25},{25,1},{2,10},{10... | collective-permute-start | bytes 491528 | tf_op jit(solution)/shard_map/ppermute | solution.py:152
  80.6 45.2 %collective-permute-start.5 = (bf16[160,512]{1,0:T(8,128)(2,1)}, bf16[160,512]{1,0:T(8,128)(2,1)}, u32[]{:S(2)}, u32[]{:S(2)}) collective-permute-start(bf16[160,512]{1,0:T(8,128)(2,1)} %bitcast.115), channel_id=1, source_target_pairs={{0,24},{8,0},{16,8},{24,16},{1,25},{9,1},{17,9},{25,17},{2,26},{10... | collective-permute-start | bytes 491528 | tf_op jit(solution)/shard_map/ppermute | solution.py:152
  97.7 33.8 %all-to-all-start = ((bf16[8,20,6144]{2,1,0:T(8,128)(2,1)}), bf16[8,20,6144]{2,1,0:T(8,128)(2,1)}, u32[]{:S(2)}, u32[]{:S(2)}) async-start(bf16[8,20,6144]{2,1,0:T(8,128)(2,1)} %convolution_convert_fusion.1), calls=%async_computation | async-start | bytes 4718592 | tf_op jit(solution)/shard_map/all_to_all | solution.py:122
  102.0 50.0 %all-gather.11.cloned.1.call-start = ((), (), s32[]{:S(2)}) async-start(), calls=%async_computation.2 | async-start | bytes 2457600 | tf_op jit(solution)/shard_map/all_gather | solution.py:130
  119.5 4.1 %copy-start.7 = (bf16[4,20,8,128]{3,2,1,0:T(8,128)(2,1)S(1)}, bf16[4,20,8,128]{3,2,1,0:T(8,128)(2,1)}, u32[]{:S(2)}) copy-start(bf16[4,20,8,128]{3,2,1,0:T(8,128)(2,1)} %copy-done.6) | copy-start | bytes 491524
  130.0 3.6 %copy-start.5 = (f32[20,6144]{1,0:T(8,128)S(1)}, f32[20,6144]{1,0:T(8,128)}, u32[]{:S(2)}) copy-start(f32[20,6144]{1,0:T(8,128)} %get-tuple-element.43) | copy-start | bytes 1474564
  130.0 3.8 %copy-start.3 = (f32[20,6144]{1,0:T(8,128)S(1)}, f32[20,6144]{1,0:T(8,128)}, u32[]{:S(2)}) copy-start(f32[20,6144]{1,0:T(8,128)} %copy-done.2) | copy-start | bytes 1474564
  130.0 14.8 %copy-start.4 = (bf16[1,128,6144]{2,1,0:T(8,128)(2,1)S(1)}, bf16[1,128,6144]{2,1,0:T(8,128)(2,1)}, u32[]{:S(2)}) copy-start(bf16[1,128,6144]{2,1,0:T(8,128)(2,1)} %param.11) | copy-start | bytes 4718596
  142.8 8.0 %collective-permute-start.8 = (f32[6144]{0:T(1024)S(1)}, f32[6144]{0:T(1024)S(1)}, u32[]{:S(2)}, u32[]{:S(2)}) collective-permute-start(f32[6144]{0:T(1024)S(1)} %reduce_sum.108), channel_id=1, source_target_pairs={{0,24},{8,0},{16,8},{24,16},{1,25},{9,1},{17,9},{25,17},{2,26},{10... | collective-permute-start | bytes 73736 | tf_op jit(solution)/shard_map/ppermute | solution.py:165
  143.5 6.9 %collective-permute-start.7 = (f32[6144]{0:T(1024)S(1)}, f32[6144]{0:T(1024)S(1)}, u32[]{:S(2)}, u32[]{:S(2)}) collective-permute-start(f32[6144]{0:T(1024)S(1)} %reduce_sum.108), channel_id=1, source_target_pairs={{0,16},{8,24},{16,0},{24,8},{1,17},{9,25},{17,1},{25,9},{2,18},{10... | collective-permute-start | bytes 73736 | tf_op jit(solution)/shard_map/ppermute | solution.py:165
  144.4 5.6 %collective-permute-start.6 = (f32[6144]{0:T(1024)S(1)}, f32[6144]{0:T(1024)S(1)}, u32[]{:S(2)}, u32[]{:S(2)}) collective-permute-start(f32[6144]{0:T(1024)S(1)} %reduce_sum.108), channel_id=1, source_target_pairs={{0,8},{8,16},{16,24},{24,0},{1,9},{9,17},{17,25},{25,1},{2,10},{10... | collective-permute-start | bytes 73736 | tf_op jit(solution)/shard_map/ppermute | solution.py:165
  152.1 8.4 %copy-start.1 = (bf16[1,128,6144]{2,1,0:T(8,128)(2,1)S(1)}, bf16[1,128,6144]{2,1,0:T(8,128)(2,1)}, u32[]{:S(2)}) copy-start(bf16[1,128,6144]{2,1,0:T(8,128)(2,1)} %param.12) | copy-start | bytes 4718596
Sparse Core Ops, SparseCore 0:
  15.8 41.8 all-gather.12
  60.1 35.6 all-gather.8
  104.5 42.7 all-gather.10
